TPU v7x, 128 devices: a whole 4x4x4 slice. The times are simulated.
128 devices in a mesh: chan: 4 (over z_lo, core), blk: 32 (over z_hi, y, x).
Axes of the slice: x: 4, y: 4, z: 4 (z_hi: 2, z_lo: 2; z = z_hi * 2 + z_lo), core: 2. Of those that a mesh axis runs over, the one named last changes fastest.
Arguments:
- voltages: bfloat16 [256, 262144], P('blk', 'chan'), may hold values from -6 to 6
- fir_taps: float32 [8, 4096], replicated, may hold values from -2.1 to 2.1
Outputs:
- visibilities: float32 [2, 256, 256, 2048], P(None, 'blk', None, 'chan')
All inputs are finite; a program needn't handle non-finite values.
Results may differ from a plain program's by a relative error of at most 0.0036.
Values may be sent and summed in bfloat16 or wider, within the bound.
No kernel may reach another device: no remote copies, remote signals or barrier semaphores. Data moves between devices by JAX's collectives and lax.ppermute only.
A program may use at most 192 MiB of HBM per device.

v0:
```python
import math
import jax
import jax.numpy as jnp
from jax import lax
from jax.experimental.layout import Layout, with_layout_constraint
from jax.sharding import PartitionSpec as P

TAPS = 8
L = 4096
C = 2048


def shifted(value, axis, steps):
    count = lax.axis_size(axis)
    leading, last = (max(0, -steps), min(count, count - steps))
    return lax.ppermute(value, axis, [(source, source + steps) for source in range(leading, last)])


def dft_table(first_channel, channel_count, length):
    channel_ids = first_channel + jnp.arange(channel_count, dtype=jnp.int32)
    sample_ids = jnp.arange(length, dtype=jnp.int32)
    phase_index = sample_ids[:, None] * channel_ids[None, :] % length
    angles = phase_index.astype(jnp.float32) * (2.0 * math.pi / length)
    normaliser = 1.0 / math.sqrt(length)
    return jnp.concatenate([jnp.cos(angles) * normaliser, -jnp.sin(angles) * normaliser], axis=1)


def correlate(own_block, every_block, inverse_count):
    real_part, imag_part = (own_block[:, 0], own_block[:, 1])
    paired = jnp.stack(
        [jnp.stack([real_part, imag_part], axis=1), jnp.stack([imag_part, -real_part], axis=1)]
    )
    products = jnp.einsum(
        "riptc,jptc->rijc", paired, every_block, preferred_element_type=jnp.float32
    )
    return products * inverse_count


def on_device(voltages, fir_taps):
    feed_count = voltages.shape[0]
    frame_count = voltages.shape[1] // L
    own_frames = voltages.reshape(feed_count, frame_count, L)
    last_frames = own_frames[:, frame_count - (TAPS - 1) :, :]
    earlier = shifted(last_frames, "chan", 1)
    extended = jnp.concatenate([earlier, own_frames], axis=1)
    filtered = jnp.zeros((feed_count, frame_count, L), jnp.float32)
    for tap_index in range(TAPS):
        filtered = filtered + fir_taps[tap_index][None, None, :] * extended[
            :, tap_index : tap_index + frame_count, :
        ].astype(jnp.float32)
    frame_rows = filtered.reshape(feed_count * frame_count, L)
    block_width = min(C, 512)
    pieces = []
    for first_channel in range(0, C, block_width):
        cos_sin_table = dft_table(first_channel, block_width, L)
        product = jnp.dot(
            frame_rows,
            cos_sin_table,
            precision=lax.Precision.HIGHEST,
            preferred_element_type=jnp.float32,
        )
        pieces.append(product.reshape(feed_count * frame_count, 2, block_width))
    spectra = (
        jnp.concatenate(pieces, axis=2).astype(jnp.bfloat16).reshape(feed_count, frame_count, 2, C)
    )
    own_block = lax.all_to_all(spectra, "chan", split_axis=3, concat_axis=1, tiled=True)
    inverse_count = 1.0 / own_block.shape[1]
    own_block = own_block.transpose(0, 2, 1, 3)
    row_major = Layout(major_to_minor=tuple(range(own_block.ndim + 1)))
    local = with_layout_constraint(own_block[None], row_major)
    gathered = with_layout_constraint(lax.all_gather(local, "blk", axis=0, tiled=True), row_major)
    every_block = gathered.reshape((-1,) + own_block.shape[1:])
    return correlate(own_block, every_block, inverse_count)


def solution(mesh):
    placed = (P("blk", "chan"), P())
    return jax.shard_map(
        on_device,
        mesh=mesh,
        in_specs=placed,
        out_specs=P(None, "blk", None, "chan"),
        check_vma=False,
    )
```

profile of v0, /device:TPU:0, one launch (start us, length us, event | category | flops | bytes accessed | tf_op | source)
XLA Modules:
  0.0 691.3 jit_solution(8309814555249872896)
XLA Ops:
  10.6 33.0 %negate_multiply_fusion.3 = (f32[4096,512]{0,1:T(8,128)S(1)}, f32[4096,512]{0,1:T(8,128)S(1)}) fusion(), kind=kLoop, calls=%fused_computation.42 | loop fusion | flops 35651584 | bytes 16777216 | tf_op jit(solution)/shard_map/mul | solution.py:25
  43.7 33.8 %cosine_multiply_fusion = (f32[4096,512]{0,1:T(8,128)S(1)}, f32[4096,512]{0,1:T(8,128)S(1)}) fusion(s32[512]{0:T(512)S(1)} %iota_add_fusion), kind=kLoop, calls=%fused_computation.31 | loop fusion | flops 35651584 | bytes 16779264 | tf_op jit(solution)/shard_map/mul | solution.py:25
  77.5 37.2 %cosine_multiply_fusion.1 = (f32[4096,512]{0,1:T(8,128)}, f32[4096,512]{0,1:T(8,128)}) fusion(s32[512]{0:T(512)S(1)} %iota_add_fusion.1), kind=kLoop, calls=%fused_computation.35 | loop fusion | flops 35651584 | bytes 16779264 | tf_op jit(solution)/shard_map/mul | solution.py:25
  114.7 37.2 %cosine_multiply_fusion.2 = (f32[4096,512]{0,1:T(8,128)}, f32[4096,512]{0,1:T(8,128)}) fusion(s32[512]{0:T(512)S(1)} %iota_add_fusion.2), kind=kLoop, calls=%fused_computation.39 | loop fusion | flops 35651584 | bytes 16779264 | tf_op jit(solution)/shard_map/mul | solution.py:25
  151.9 6.4 pad_maximum_fusion.3
  158.3 13.7 %pad_maximum_fusion.2 = f32[4096,1024]{0,1:T(8,128)} fusion(f32[4096,512]{0,1:T(8,128)} %get-tuple-element.18, f32[4096,512]{0,1:T(8,128)} %get-tuple-element.17), kind=kLoop, calls=%fused_computation.2 | loop fusion | flops 4194304 | bytes 33554432 | tf_op jit(solution)/shard_map/concatenate | solution.py:25
  172.0 2.7 copy-done.1
  174.8 6.6 pad_maximum_fusion.1
  181.3 6.4 pad_maximum_fusion
  187.8 5.6 multiply_add_fusion
  193.5 22.5 %fusion.42 = bf16[8,16,2,512]{3,1,2,0:T(8,128)(2,1)} fusion(f32[2,512,4096,1]{2,1,0,3:T(8,128)} %bitcast.79, f32[8,16,4096]{2,1,0:T(8,128)S(1)} %multiply_add_fusion), kind=kOutput, calls=%fused_computation.75 | convolution fusion | flops 6442582016 | bytes 19136512 | tf_op jit(solution)/shard_map/dot_general | solution.py:56
  216.0 20.0 %fusion.39 = bf16[8,16,2,512]{3,1,2,0:T(8,128)(2,1)} fusion(f32[2,512,4096,1]{2,1,0,3:T(8,128)S(1)} %bitcast.82, f32[8,16,4096]{2,1,0:T(8,128)} %copy-done.2), kind=kOutput, calls=%fused_computation.74 | convolution fusion | flops 6442582016 | bytes 19136512 | tf_op jit(solution)/shard_map/dot_general | solution.py:56
  236.0 20.8 %fusion.36 = bf16[8,16,2,512]{3,1,2,0:T(8,128)(2,1)S(1)} fusion(f32[2,512,4096,1]{2,1,0,3:T(8,128)} %bitcast.83, f32[8,16,4096]{2,1,0:T(8,128)S(1)} %copy-done.3), kind=kOutput, calls=%fused_computation.73 | convolution fusion | flops 6442582016 | bytes 19136512 | tf_op jit(solution)/shard_map/dot_general | solution.py:56
  256.9 17.6 %fusion.33 = bf16[8,16,2,512]{3,1,2,0:T(8,128)(2,1)S(1)} fusion(f32[2,512,4096,1]{2,1,0,3:T(8,128)S(1)} %bitcast.86, f32[8,16,4096]{2,1,0:T(8,128)S(1)} %copy-done.3), kind=kOutput, calls=%fused_computation.72 | convolution fusion | flops 6442582016 | bytes 19136512 | tf_op jit(solution)/shard_map/dot_general | solution.py:56
  274.6 14.3 %copy.13 = bf16[8,16,2,2048]{1,2,0,3:T(2,128)(2,1)} copy(bf16[8,16,2,2048]{3,1,2,0:T(8,128)(2,1)S(1)} %pad_maximum_fusion.6) | data formatting | bytes 2097152 | tf_op jit(solution)/shard_map/concatenate | solution.py:64
  288.9 10.2 %reshape.57 = bf16[4,2,65536]{2,1,0:T(2,128)(2,1)S(1)} reshape(bf16[2048,8,2,16]{3,2,1,0:T(2,128)(2,1)} %bitcast.76) | data formatting | bytes 2097152
  299.2 17.5 %all_to_all.18 = bf16[4,2,65536]{2,1,0:T(2,128)(2,1)S(1)} all-to-all(bf16[4,2,65536]{2,1,0:T(2,128)(2,1)S(1)} %reshape.57), channel_id=1, replica_groups=mesh['chan'=4,'blk'=32] {'chan'}, dimensions={0} | all-to-all | bytes 2097152 | tf_op jit(solution)/shard_map/all_to_all | solution.py:66
  316.6 7.1 %reshape.58 = bf16[2048,8,2,16]{3,2,1,0:T(2,128)(2,1)} reshape(bf16[4,2,65536]{2,1,0:T(2,128)(2,1)S(1)} %all_to_all.18) | data formatting | bytes 2097152
  323.7 19.3 %copy.14 = bf16[8,16,2,4,512]{4,1,3,2,0:T(8,128)(2,1)} copy(bf16[8,16,2,4,512]{1,2,0,4,3:T(2,128)(2,1)} %bitcast.77) | data formatting | bytes 2097152 | tf_op jit(solution)/shard_map/all_to_all | solution.py:66
  345.9 6.6 copy.16
  352.5 253.8 %all-gather.2.cloned.1.call-done = bf16[32,8,2,64,512]{4,3,2,1,0:T(8,128)(2,1)} async-done(((bf16[1,8,2,64,512]{4,3,2,1,0:T(8,128)(2,1)}), bf16[32,8,2,64,512]{4,3,2,1,0:T(8,128)(2,1)}) %all-gather.2.cloned.1.call-update) | async-done | bytes 33554448 | tf_op jit(solution)/shard_map/all_gather | solution.py:71
  606.3 50.8 %copy.19 = bf16[256,2,64,512,1]{0,2,1,4,3:T(8,128)(2,1)} copy(bf16[256,2,64,512,1]{3,2,1,0,4:T(8,128)(2,1)} %bitcast.78) | data formatting | bytes 67108864 | tf_op jit(solution)/shard_map/reshape | solution.py:72
  657.0 17.2 %fusion.12 = f32[2,8,256,512]{2,1,0,3:T(8,128)} fusion(bf16[256,2,64,512,1]{0,2,1,4,3:T(8,128)(2,1)} %copy.19, bf16[2,8,2,64,512]{3,1,2,0,4:T(8,128)(2,1)} %copy.16), kind=kOutput, calls=%fused_computation.29 | convolution fusion | flops 538968064 | bytes 44040192 | tf_op jit(solution)/shard_map/riptc,jptc->rijc/dot_general | solution.py:33
  674.2 9.9 %copy.17 = f32[2,8,256,512]{3,2,1,0:T(8,128)} copy(f32[2,8,256,512]{2,1,0,3:T(8,128)} %fusion.12) | data formatting | bytes 16777216 | tf_op jit(solution)/shard_map/mul | solution.py:36
  (45 shorter events, 7.2 us)
Async XLA Ops:
  6.5 599.7 %all-gather.2.cloned.1.call-start = ((), (), s32[]{:S(2)}) async-start(), calls=%async_computation.1 | async-start | bytes 34603008 | tf_op jit(solution)/shard_map/all_gather | solution.py:71
  8.5 179.3 %collective-permute-start = (bf16[8,7,4096]{2,1,0:T(8,128)(2,1)S(1)}, bf16[8,7,4096]{2,1,0:T(8,128)(2,1)}, u32[]{:S(2)}, u32[]{:S(2)}) collective-permute-start(bf16[8,7,4096]{2,1,0:T(8,128)(2,1)S(1)} %slice.73), channel_id=1, source_target_pairs={{0,32},{32,64},{64,96},{1,33},{33,65},{65,97},{2,34},{34,66},{66,9... | collective-permute-start | bytes 1376264 | tf_op jit(solution)/shard_map/ppermute | solution.py:16
  10.6 33.0 %copy-start.6 = (f32[8,4096]{1,0:T(8,128)S(1)}, f32[8,4096]{1,0:T(8,128)}, u32[]{:S(2)}) copy-start(f32[8,4096]{1,0:T(8,128)} %param.3) | copy-start | bytes 393220
  158.3 13.7 %copy-start = (f32[4096,512]{0,1:T(8,128)S(1)}, f32[4096,512]{0,1:T(8,128)}, u32[]{:S(2)}) copy-start(f32[4096,512]{0,1:T(8,128)} %get-tuple-element.15) | copy-start | bytes 25165828
  158.3 16.5 %copy-start.1 = (f32[4096,512]{0,1:T(8,128)S(1)}, f32[4096,512]{0,1:T(8,128)}, u32[]{:S(2)}) copy-start(f32[4096,512]{0,1:T(8,128)} %get-tuple-element.16) | copy-start | bytes 25165828
  187.8 28.2 %slice-start = ((s8[16777216]{0:T(1024)(128)(4,1)}), s8[4194304]{0:T(1024)(128)(4,1)S(1)}, s32[]{:S(2)}) async-start(s8[16777216]{0:T(1024)(128)(4,1)} %bitcast.80), calls=%async_computation.2 | async-start | bytes 8388608
  193.4 22.5 %copy-start.2 = (f32[8,16,4096]{2,1,0:T(8,128)}, f32[8,16,4096]{2,1,0:T(8,128)S(1)}, u32[]{:S(2)}) copy-start(f32[8,16,4096]{2,1,0:T(8,128)S(1)} %multiply_add_fusion) | copy-start | bytes 6291460
  193.4 22.5 %slice-start.1 = ((s8[16777216]{0:T(1024)(128)(4,1)}), s8[4194304]{0:T(1024)(128)(4,1)S(1)}, s32[]{:S(2)}) async-start(s8[16777216]{0:T(1024)(128)(4,1)} %bitcast.80), calls=%async_computation.3 | async-start | bytes 8388608
  193.4 22.5 %slice-start.2 = ((s8[16777216]{0:T(1024)(128)(4,1)}), s8[4194304]{0:T(1024)(128)(4,1)S(1)}, s32[]{:S(2)}) async-start(s8[16777216]{0:T(1024)(128)(4,1)} %bitcast.80), calls=%async_computation.4 | async-start | bytes 8388608
  193.4 22.5 %slice-start.3 = ((s8[16777216]{0:T(1024)(128)(4,1)}), s8[4194304]{0:T(1024)(128)(4,1)S(1)}, s32[]{:S(2)}) async-start(s8[16777216]{0:T(1024)(128)(4,1)} %bitcast.80), calls=%async_computation.5 | async-start | bytes 8388608
  216.0 20.0 %copy-start.3 = (f32[8,16,4096]{2,1,0:T(8,128)S(1)}, f32[8,16,4096]{2,1,0:T(8,128)}, u32[]{:S(2)}) copy-start(f32[8,16,4096]{2,1,0:T(8,128)} %copy-done.2) | copy-start | bytes 6291460
  216.0 40.8 %slice-start.4 = ((s8[16777216]{0:T(1024)(128)(4,1)}), s8[4194304]{0:T(1024)(128)(4,1)S(1)}, s32[]{:S(2)}) async-start(s8[16777216]{0:T(1024)(128)(4,1)} %bitcast.84), calls=%async_computation.6 | async-start | bytes 8388608
  216.0 40.8 %slice-start.5 = ((s8[16777216]{0:T(1024)(128)(4,1)}), s8[4194304]{0:T(1024)(128)(4,1)S(1)}, s32[]{:S(2)}) async-start(s8[16777216]{0:T(1024)(128)(4,1)} %bitcast.84), calls=%async_computation.7 | async-start | bytes 8388608
  236.0 20.8 %slice-start.6 = ((s8[16777216]{0:T(1024)(128)(4,1)}), s8[4194304]{0:T(1024)(128)(4,1)S(1)}, s32[]{:S(2)}) async-start(s8[16777216]{0:T(1024)(128)(4,1)} %bitcast.84), calls=%async_computation.8 | async-start | bytes 8388608
  236.0 20.8 %slice-start.7 = ((s8[16777216]{0:T(1024)(128)(4,1)}), s8[4194304]{0:T(1024)(128)(4,1)S(1)}, s32[]{:S(2)}) async-start(s8[16777216]{0:T(1024)(128)(4,1)} %bitcast.84), calls=%async_computation.9 | async-start | bytes 8388608
  256.8 17.6 %copy-start.4 = (bf16[8,16,2,512]{3,1,2,0:T(8,128)(2,1)S(1)}, bf16[8,16,2,512]{3,1,2,0:T(8,128)(2,1)}, u32[]{:S(2)}) copy-start(bf16[8,16,2,512]{3,1,2,0:T(8,128)(2,1)} %fusion.42) | copy-start | bytes 786436
  256.8 17.6 %copy-start.5 = (bf16[8,16,2,512]{3,1,2,0:T(8,128)(2,1)S(1)}, bf16[8,16,2,512]{3,1,2,0:T(8,128)(2,1)}, u32[]{:S(2)}) copy-start(bf16[8,16,2,512]{3,1,2,0:T(8,128)(2,1)} %fusion.39) | copy-start | bytes 786436
Sparse Core Ops, SparseCore 0:
  343.2 263.0 all-gather.1
where the time goes:
time: 701 us; the launch traced here: 691 us
  waiting for transfers between devices  254 us (36%)
  other arithmetic  183 us (26%)
  local copies, waits for them, and re-layouts  123 us (18%)
  matrix products  98 us (14%)
  blocking collectives  17.5 us (2%)
  between operations  14.1 us (2%)
    all_gather x1, waiting for transfers between devices, on_device(): lax.all_gather(local, 'blk', axis=0, tiled=True)  254 us
    mul x3, other arithmetic, dft_table(): jnp.cos(angles) * normaliser  108 us
    dot_general x4, matrix products, on_device(): jnp.dot(frame_rows, cos_sin_table, precision=lax.Precision.HIGHEST, prefe...  80.8 us
    reshape x1, local copies, waits for them, and re-layouts, on_device(): every_block = gathered.reshape((-1,) + own_block.shape[1:])  50.8 us
    concatenate x4, other arithmetic, dft_table(): jnp.concatenate([jnp.cos(angles) * normaliser, -jnp.sin(angles) * normali...  33.1 us
    mul x1, other arithmetic, dft_table(): -jnp.sin(angles) * normaliser  33 us
    unnamed x32, local copies, waits for them, and re-layouts  20.1 us
    all_to_all x1, local copies, waits for them, and re-layouts, on_device(): lax.all_to_all(spectra, 'chan', split_axis=3, concat_axis=1, tiled=True)  19.3 us
  transfers between devices with their start and end apart: 2, of which 1 were waited for; matrix products, arithmetic and copies ran while one was open for 27% of the time, Pallas kernels for 0%

commit v1 on v0

--- a/solution.py
+++ b/solution.py
@@ -1,3 +1,4 @@
+import functools
 import math
 import jax
 import jax.numpy as jnp
@@ -8,6 +9,22 @@
 TAPS = 8
 L = 4096
 C = 2048
+
+
+def samples_all_test(my_data, dev_axis):
+    work_now = jnp.concatenate(
+        lax.all_to_all(
+            jnp.stack(jnp.split(my_data, lax.axis_size(dev_axis), axis=3), axis=0),
+            axis_name=dev_axis,
+            split_axis=0,
+            concat_axis=0,
+        ),
+        axis=1,
+    )
+    return work_now
+
+
+_set_steps_all = functools.partial(samples_all_test, dev_axis="chan")
 
 
 def shifted(value, axis, steps):
@@ -63,7 +80,7 @@
     spectra = (
         jnp.concatenate(pieces, axis=2).astype(jnp.bfloat16).reshape(feed_count, frame_count, 2, C)
     )
-    own_block = lax.all_to_all(spectra, "chan", split_axis=3, concat_axis=1, tiled=True)
+    own_block = _set_steps_all(spectra)
     inverse_count = 1.0 / own_block.shape[1]
     own_block = own_block.transpose(0, 2, 1, 3)
     row_major = Layout(major_to_minor=tuple(range(own_block.ndim + 1)))

time: 701 us -> 650 us (0.927)
  local copies, waits for them, and re-layouts: 123 us -> 73.2 us
    all_to_all x1 -> x0, local copies, waits for them, and re-layouts: 19.3 us -> none  [on_device(): lax.all_to_all(spectra, 'chan', split_axis=3, concat_axis=1, tiled=True)]
    unnamed x32 -> x30, local copies, waits for them, and re-layouts: 20.1 us -> 2.81 us
    concatenate x1 -> x0, local copies, waits for them, and re-layouts: 14.3 us -> none  [on_device(): jnp.concatenate(pieces, axis=2).astype(jnp.bfloat16)]
  transfers between devices with their start and end apart: 2 -> 2, of which waited for: 1 -> 1; matrix products, arithmetic and copies ran while one was open for 27% -> 29% of each run, Pallas kernels for 0% -> 0%
where the time goes in v1:
time: 650 us; the launch traced here: 641 us
  waiting for transfers between devices  254 us (39%)
  other arithmetic  183 us (28%)
  matrix products  98 us (15%)
  local copies, waits for them, and re-layouts  73.2 us (11%)
  blocking collectives  17.5 us (3%)
  between operations  13.9 us (2%)
    all_gather x1, waiting for transfers between devices, on_device(): lax.all_gather(local, 'blk', axis=0, tiled=True)  254 us
    mul x3, other arithmetic, dft_table(): jnp.cos(angles) * normaliser  108 us
    dot_general x4, matrix products, on_device(): jnp.dot(frame_rows, cos_sin_table, precision=lax.Precision.HIGHEST, prefe...  80.8 us
    reshape x1, local copies, waits for them, and re-layouts, on_device(): every_block = gathered.reshape((-1,) + own_block.shape[1:])  50.8 us
    concatenate x4, other arithmetic, dft_table(): jnp.concatenate([jnp.cos(angles) * normaliser, -jnp.sin(angles) * normali...  33.4 us
    mul x1, other arithmetic, dft_table(): -jnp.sin(angles) * normaliser  33 us
    all_to_all x1, blocking collectives, samples_all_test(): lax.all_to_all(jnp.stack(jnp.split(my_data, lax.axis_size(dev_axis), axis...  17.5 us
    dot_general x1, matrix products, correlate(): jnp.einsum('riptc,jptc->rijc', paired, every_block, preferred_element_typ...  17.2 us
  transfers between devices with their start and end apart: 2, of which 1 were waited for; matrix products, arithmetic and copies ran while one was open for 29% of the time, Pallas kernels for 0%

profile of v1, /device:TPU:0, one launch (start us, length us, event | category | flops | bytes accessed | tf_op | source)
XLA Modules:
  0.0 641.4 jit_solution(15346167007774536682)
XLA Ops:
  6.5 1.8 copy.10
  8.5 2.1 collective-permute-start
  10.6 33.0 %negate_multiply_fusion.3 = (f32[4096,512]{0,1:T(8,128)S(1)}, f32[4096,512]{0,1:T(8,128)S(1)}) fusion(), kind=kLoop, calls=%fused_computation.42 | loop fusion | flops 35651584 | bytes 16777216 | tf_op jit(solution)/shard_map/mul | solution.py:42
  43.7 33.6 %cosine_multiply_fusion = (f32[4096,512]{0,1:T(8,128)S(1)}, f32[4096,512]{0,1:T(8,128)S(1)}) fusion(s32[512]{0:T(512)S(1)} %iota_add_fusion), kind=kLoop, calls=%fused_computation.31 | loop fusion | flops 35651584 | bytes 16779264 | tf_op jit(solution)/shard_map/mul | solution.py:42
  77.3 37.2 %cosine_multiply_fusion.1 = (f32[4096,512]{0,1:T(8,128)}, f32[4096,512]{0,1:T(8,128)}) fusion(s32[512]{0:T(512)S(1)} %iota_add_fusion.1), kind=kLoop, calls=%fused_computation.35 | loop fusion | flops 35651584 | bytes 16779264 | tf_op jit(solution)/shard_map/mul | solution.py:42
  114.5 37.2 %cosine_multiply_fusion.2 = (f32[4096,512]{0,1:T(8,128)}, f32[4096,512]{0,1:T(8,128)}) fusion(s32[512]{0:T(512)S(1)} %iota_add_fusion.2), kind=kLoop, calls=%fused_computation.39 | loop fusion | flops 35651584 | bytes 16779264 | tf_op jit(solution)/shard_map/mul | solution.py:42
  151.8 6.4 pad_maximum_fusion.3
  158.1 13.7 %pad_maximum_fusion.2 = f32[4096,1024]{0,1:T(8,128)} fusion(f32[4096,512]{0,1:T(8,128)} %get-tuple-element.18, f32[4096,512]{0,1:T(8,128)} %get-tuple-element.17), kind=kLoop, calls=%fused_computation.2 | loop fusion | flops 4194304 | bytes 33554432 | tf_op jit(solution)/shard_map/concatenate | solution.py:42
  171.9 2.7 copy-done.1
  174.6 6.9 %pad_maximum_fusion.1 = f32[4096,1024]{0,1:T(8,128)} fusion(f32[4096,512]{0,1:T(8,128)S(1)} %copy-done.1, f32[4096,512]{0,1:T(8,128)S(1)} %copy-done), kind=kLoop, calls=%fused_computation.1 | loop fusion | flops 4194304 | bytes 33554432 | tf_op jit(solution)/shard_map/concatenate | solution.py:42
  181.5 6.4 %pad_maximum_fusion = f32[4096,1024]{0,1:T(8,128)} fusion(f32[4096,512]{0,1:T(8,128)S(1)} %get-tuple-element.21, f32[4096,512]{0,1:T(8,128)S(1)} %get-tuple-element.22), kind=kLoop, calls=%fused_computation | loop fusion | flops 4194304 | bytes 33554432 | tf_op jit(solution)/shard_map/concatenate | solution.py:42
  187.9 5.6 multiply_add_fusion
  193.6 22.3 %fusion.45 = bf16[1,8,16,2,512]{4,2,3,1,0:T(8,128)(2,1)} fusion(f32[2,512,4096,1]{2,1,0,3:T(8,128)} %bitcast.89, f32[8,16,4096]{2,1,0:T(8,128)S(1)} %multiply_add_fusion), kind=kOutput, calls=%fused_computation.76 | convolution fusion | flops 6442582016 | bytes 19136512 | tf_op jit(solution)/shard_map/dot_general | solution.py:73
  216.0 20.2 %fusion.48 = bf16[1,8,16,2,512]{4,2,3,1,0:T(8,128)(2,1)} fusion(f32[2,512,4096,1]{2,1,0,3:T(8,128)S(1)} %bitcast.92, f32[8,16,4096]{2,1,0:T(8,128)} %copy-done.2), kind=kOutput, calls=%fused_computation.77 | convolution fusion | flops 6442582016 | bytes 19136512 | tf_op jit(solution)/shard_map/dot_general | solution.py:73
  236.2 20.8 %fusion.51 = bf16[1,8,16,2,512]{4,2,3,1,0:T(8,128)(2,1)S(1)} fusion(f32[2,512,4096,1]{2,1,0,3:T(8,128)} %bitcast.93, f32[8,16,4096]{2,1,0:T(8,128)S(1)} %copy-done.3), kind=kOutput, calls=%fused_computation.78 | convolution fusion | flops 6442582016 | bytes 19136512 | tf_op jit(solution)/shard_map/dot_general | solution.py:73
  257.0 17.6 %fusion.54 = bf16[1,8,16,2,512]{4,2,3,1,0:T(8,128)(2,1)S(1)} fusion(f32[2,512,4096,1]{2,1,0,3:T(8,128)S(1)} %bitcast.96, f32[8,16,4096]{2,1,0:T(8,128)S(1)} %copy-done.3), kind=kOutput, calls=%fused_computation.79 | convolution fusion | flops 6442582016 | bytes 19136512 | tf_op jit(solution)/shard_map/dot_general | solution.py:73
  274.8 17.5 %all_to_all.5 = bf16[4,8,16,2,512]{4,2,3,1,0:T(8,128)(2,1)S(1)} all-to-all(bf16[4,8,16,2,512]{4,2,3,1,0:T(8,128)(2,1)S(1)} %pad_maximum_fusion.6), channel_id=1, replica_groups=mesh['chan'=4,'blk'=32] {'chan'}, dimensions={0} | all-to-all | bytes 2097152 | tf_op jit(solution)/shard_map/all_to_all | solution.py:16
  293.3 1.3 fusion.63
  294.7 1.4 pad_maximum_fusion.4
  296.2 6.6 %copy.15 = bf16[2,8,2,64,512]{3,1,2,0,4:T(8,128)(2,1)} copy(bf16[2,8,2,64,512]{4,3,2,1,0:T(8,128)(2,1)S(1)} %pad_maximum_fusion.4) | data formatting | bytes 4194304 | tf_op jit(solution)/shard_map/stack | solution.py:47
  302.8 253.7 %all-gather.2.cloned.1.call-done = bf16[32,8,2,64,512]{4,3,2,1,0:T(8,128)(2,1)} async-done(((bf16[1,8,2,64,512]{4,3,2,1,0:T(8,128)(2,1)}), bf16[32,8,2,64,512]{4,3,2,1,0:T(8,128)(2,1)}) %all-gather.2.cloned.1.call-update) | async-done | bytes 33554448 | tf_op jit(solution)/shard_map/all_gather | solution.py:88
  556.5 50.8 %copy.18 = bf16[256,2,64,512,1]{0,2,1,4,3:T(8,128)(2,1)} copy(bf16[256,2,64,512,1]{3,2,1,0,4:T(8,128)(2,1)} %bitcast.88) | data formatting | bytes 67108864 | tf_op jit(solution)/shard_map/reshape | solution.py:89
  607.3 17.2 %fusion.12 = f32[2,8,256,512]{2,1,0,3:T(8,128)} fusion(bf16[256,2,64,512,1]{0,2,1,4,3:T(8,128)(2,1)} %copy.18, bf16[2,8,2,64,512]{3,1,2,0,4:T(8,128)(2,1)} %copy.15), kind=kOutput, calls=%fused_computation.29 | convolution fusion | flops 538968064 | bytes 44040192 | tf_op jit(solution)/shard_map/riptc,jptc->rijc/dot_general | solution.py:50
  624.5 9.9 %copy.16 = f32[2,8,256,512]{3,2,1,0:T(8,128)} copy(f32[2,8,256,512]{2,1,0,3:T(8,128)} %fusion.12) | data formatting | bytes 16777216 | tf_op jit(solution)/shard_map/mul | solution.py:53
  (42 shorter events, 1.6 us)
Async XLA Ops:
  6.5 550.0 %all-gather.2.cloned.1.call-start = ((), (), s32[]{:S(2)}) async-start(), calls=%async_computation.1 | async-start | bytes 34603008 | tf_op jit(solution)/shard_map/all_gather | solution.py:88
  8.5 179.5 %collective-permute-start = (bf16[8,7,4096]{2,1,0:T(8,128)(2,1)S(1)}, bf16[8,7,4096]{2,1,0:T(8,128)(2,1)}, u32[]{:S(2)}, u32[]{:S(2)}) collective-permute-start(bf16[8,7,4096]{2,1,0:T(8,128)(2,1)S(1)} %slice.73), channel_id=1, source_target_pairs={{0,32},{32,64},{64,96},{1,33},{33,65},{65,97},{2,34},{34,66},{66,9... | collective-permute-start | bytes 1376264 | tf_op jit(solution)/shard_map/ppermute | solution.py:33
  10.6 33.0 %copy-start.6 = (f32[8,4096]{1,0:T(8,128)S(1)}, f32[8,4096]{1,0:T(8,128)}, u32[]{:S(2)}) copy-start(f32[8,4096]{1,0:T(8,128)} %param.3) | copy-start | bytes 393220
  158.1 13.7 %copy-start = (f32[4096,512]{0,1:T(8,128)S(1)}, f32[4096,512]{0,1:T(8,128)}, u32[]{:S(2)}) copy-start(f32[4096,512]{0,1:T(8,128)} %get-tuple-element.15) | copy-start | bytes 25165828
  158.1 16.5 %copy-start.1 = (f32[4096,512]{0,1:T(8,128)S(1)}, f32[4096,512]{0,1:T(8,128)}, u32[]{:S(2)}) copy-start(f32[4096,512]{0,1:T(8,128)} %get-tuple-element.16) | copy-start | bytes 25165828
  187.9 28.0 %slice-start = ((s8[16777216]{0:T(1024)(128)(4,1)}), s8[4194304]{0:T(1024)(128)(4,1)S(1)}, s32[]{:S(2)}) async-start(s8[16777216]{0:T(1024)(128)(4,1)} %bitcast.90), calls=%async_computation.2 | async-start | bytes 8388608
  193.6 22.3 %copy-start.2 = (f32[8,16,4096]{2,1,0:T(8,128)}, f32[8,16,4096]{2,1,0:T(8,128)S(1)}, u32[]{:S(2)}) copy-start(f32[8,16,4096]{2,1,0:T(8,128)S(1)} %multiply_add_fusion) | copy-start | bytes 6291460
  193.6 22.3 %slice-start.1 = ((s8[16777216]{0:T(1024)(128)(4,1)}), s8[4194304]{0:T(1024)(128)(4,1)S(1)}, s32[]{:S(2)}) async-start(s8[16777216]{0:T(1024)(128)(4,1)} %bitcast.90), calls=%async_computation.3 | async-start | bytes 8388608
  193.6 22.3 %slice-start.2 = ((s8[16777216]{0:T(1024)(128)(4,1)}), s8[4194304]{0:T(1024)(128)(4,1)S(1)}, s32[]{:S(2)}) async-start(s8[16777216]{0:T(1024)(128)(4,1)} %bitcast.90), calls=%async_computation.4 | async-start | bytes 8388608
  193.6 22.3 %slice-start.3 = ((s8[16777216]{0:T(1024)(128)(4,1)}), s8[4194304]{0:T(1024)(128)(4,1)S(1)}, s32[]{:S(2)}) async-start(s8[16777216]{0:T(1024)(128)(4,1)} %bitcast.90), calls=%async_computation.5 | async-start | bytes 8388608
  216.0 20.2 %copy-start.3 = (f32[8,16,4096]{2,1,0:T(8,128)S(1)}, f32[8,16,4096]{2,1,0:T(8,128)}, u32[]{:S(2)}) copy-start(f32[8,16,4096]{2,1,0:T(8,128)} %copy-done.2) | copy-start | bytes 6291460
  216.0 41.0 %slice-start.4 = ((s8[16777216]{0:T(1024)(128)(4,1)}), s8[4194304]{0:T(1024)(128)(4,1)S(1)}, s32[]{:S(2)}) async-start(s8[16777216]{0:T(1024)(128)(4,1)} %bitcast.94), calls=%async_computation.6 | async-start | bytes 8388608
  216.0 41.0 %slice-start.5 = ((s8[16777216]{0:T(1024)(128)(4,1)}), s8[4194304]{0:T(1024)(128)(4,1)S(1)}, s32[]{:S(2)}) async-start(s8[16777216]{0:T(1024)(128)(4,1)} %bitcast.94), calls=%async_computation.7 | async-start | bytes 8388608
  236.2 20.8 %slice-start.6 = ((s8[16777216]{0:T(1024)(128)(4,1)}), s8[4194304]{0:T(1024)(128)(4,1)S(1)}, s32[]{:S(2)}) async-start(s8[16777216]{0:T(1024)(128)(4,1)} %bitcast.94), calls=%async_computation.8 | async-start | bytes 8388608
  236.2 20.8 %slice-start.7 = ((s8[16777216]{0:T(1024)(128)(4,1)}), s8[4194304]{0:T(1024)(128)(4,1)S(1)}, s32[]{:S(2)}) async-start(s8[16777216]{0:T(1024)(128)(4,1)} %bitcast.94), calls=%async_computation.9 | async-start | bytes 8388608
  257.0 17.6 %copy-start.4 = (bf16[1,8,16,2,512]{4,2,3,1,0:T(8,128)(2,1)S(1)}, bf16[1,8,16,2,512]{4,2,3,1,0:T(8,128)(2,1)}, u32[]{:S(2)}) copy-start(bf16[1,8,16,2,512]{4,2,3,1,0:T(8,128)(2,1)} %fusion.45) | copy-start | bytes 786436
  257.0 17.6 %copy-start.5 = (bf16[1,8,16,2,512]{4,2,3,1,0:T(8,128)(2,1)S(1)}, bf16[1,8,16,2,512]{4,2,3,1,0:T(8,128)(2,1)}, u32[]{:S(2)}) copy-start(bf16[1,8,16,2,512]{4,2,3,1,0:T(8,128)(2,1)} %fusion.48) | copy-start | bytes 786436
Sparse Core Ops, SparseCore 0:
  293.5 263.0 all-gather.1
